TPU v7x, 32 devices: a whole 2x2x4 slice. The times are simulated.
32 devices in a mesh: groups: 2 (over y), tensor: 4 (over x, core), dp: 4 (over z).
Axes of the slice: x: 2, y: 2, z: 4, core: 2. Of those that a mesh axis runs over, the one named last changes fastest.
Arguments:
- tokens: bfloat16 [65536, 4096], P(('groups', 'dp'), 'tensor'), parts along dimension 0, may hold values from -6 to 6
- cotangent: bfloat16 [65536, 4096], P(('groups', 'dp'), 'tensor'), parts along dimension 0, may hold values from -6 to 6
- w_first: bfloat16 [16, 256, 256], P('tensor'), may hold values from -0.375 to 0.375
- w_second: bfloat16 [16, 256, 256], P('tensor'), may hold values from -0.375 to 0.375
Outputs:
- grad_tokens: bfloat16 [65536, 4096], P(('groups', 'dp'), 'tensor'), parts along dimension 0
- grad_first: float32 [32, 256, 256], P(('groups', 'tensor'), 'dp'), parts along dimension 0
- grad_second: float32 [32, 256, 256], P(('groups', 'tensor'), 'dp'), parts along dimension 0
There are 2 independent parts, one for each index of `groups`. A program takes and returns all parts, laid end to end along the dimension named above; an argument that names none is the same for every part. Nothing has to cross between parts.
All inputs are finite; a program needn't handle non-finite values.
Results may differ from a plain program's by a relative error of at most 0.0065.
Values may be sent and summed in bfloat16 or wider, within the bound.
No kernel may reach another device: no remote copies, remote signals or barrier semaphores. Data moves between devices by JAX's collectives and lax.ppermute only.
A program may use at most 192 MiB of HBM per device.

v0:
```python
import math
import jax
import jax.numpy as jnp
from jax import lax
from jax.sharding import PartitionSpec as P

NB = 16


def shards(tokens, cotangent, w_first, w_second):
    tok_rows = tokens.shape[0]
    blk_local = w_first.shape[0]
    blk_width = w_first.shape[1]
    sub_width = blk_width // NB
    dp_count = lax.axis_size("dp")
    grad_scale = 1.0 / math.sqrt(tok_rows * dp_count)
    inputs = tokens.reshape(tok_rows, blk_local, blk_width)
    upstream = cotangent.reshape(tok_rows, blk_local, blk_width)
    hidden = jnp.einsum("tbi,bij->bjt", inputs, w_first, preferred_element_type=jnp.float32).astype(
        jnp.bfloat16
    )
    hidden = hidden.reshape(blk_local, NB, sub_width, tok_rows)
    second_view = w_second.reshape(blk_local, sub_width, NB, blk_width)
    moved = lax.all_to_all(hidden, "tensor", split_axis=1, concat_axis=0, tiled=True)
    active = jnp.maximum(moved, jnp.zeros((), jnp.bfloat16))
    second_term = jnp.einsum("bcjt,tco->cjbo", active, upstream, preferred_element_type=jnp.float32)
    second_term = second_term.reshape(blk_local, blk_width, blk_width) * grad_scale
    backed = jnp.einsum("tco,cjbo->bcjt", upstream, second_view, preferred_element_type=jnp.float32)
    masked = jnp.where(moved > 0, backed, jnp.zeros((), jnp.float32)).astype(jnp.bfloat16)
    returned = lax.all_to_all(masked, "tensor", split_axis=0, concat_axis=1, tiled=True)
    returned = returned.reshape(blk_local, blk_width, tok_rows)
    first_term = (
        jnp.einsum("tbi,bjt->bij", inputs, returned, preferred_element_type=jnp.float32)
        * grad_scale
    )
    grad_tokens = jnp.einsum("bjt,bij->tbi", returned, w_first, preferred_element_type=jnp.float32)
    grad_tokens = grad_tokens.astype(jnp.bfloat16).reshape(tok_rows, blk_local * blk_width)
    grad_first, grad_second = (
        lax.psum_scatter(first_term, "dp", scatter_dimension=1, tiled=True),
        lax.psum_scatter(second_term, "dp", scatter_dimension=1, tiled=True),
    )
    return (grad_tokens, grad_first, grad_second)


def solution(mesh):
    return jax.shard_map(
        shards,
        mesh=mesh,
        in_specs=(
            P(("groups", "dp"), "tensor"),
            P(("groups", "dp"), "tensor"),
            P("tensor", None, None),
            P("tensor", None, None),
        ),
        out_specs=(
            P(("groups", "dp"), "tensor"),
            P(("groups", "tensor"), "dp", None),
            P(("groups", "tensor"), "dp", None),
        ),
        check_vma=False,
    )
```

profile of v0, /device:TPU:0, one launch (start us, length us, event | category | flops | bytes accessed | tf_op | source)
XLA Modules:
  0.0 638.0 jit_solution(12787721479795042683)
XLA Ops:
  7.2 0.0 copy-start
  7.2 1.0 copy-done
  8.2 20.5 %fusion.5 = bf16[4,256,8192]{2,1,0:T(8,128)(2,1)} fusion(bf16[4,256,256]{2,1,0:T(8,128)(2,1)S(1)} %copy-done, bf16[1024,4,8,256]{3,2,1,0:T(8,128)(2,1)} %bitcast.56), kind=kOutput, calls=%fused_computation.7 | convolution fusion | flops 4303355904 | bytes 34078720 | tf_op jit(solution)/shard_map/tbi,bij->bjt/dot_general | solution.py:19
  28.8 13.9 %copy.30 = bf16[4,16,16,8192]{3,2,0,1:T(8,128)(2,1)} copy(bf16[4,16,16,8192]{3,2,1,0:T(8,128)(2,1)} %bitcast.53) | data formatting | bytes 33554432 | tf_op jit(solution)/shard_map/reshape | solution.py:22
  42.6 7.0 %all-to-all-start = ((bf16[4,16,16,8192]{3,2,0,1:T(8,128)(2,1)}), bf16[4,16,16,8192]{3,2,0,1:T(8,128)(2,1)}, u32[]{:S(2)}, u32[]{:S(2)}) async-start(bf16[4,16,16,8192]{3,2,0,1:T(8,128)(2,1)} %copy.30), calls=%async_computation | async-start | bytes 33554432 | tf_op jit(solution)/shard_map/all_to_all | solution.py:24
  49.6 27.9 %reshape.39 = bf16[8192,4,256]{2,1,0:T(4,128)(2,1)} reshape(bf16[8192,1024]{1,0:T(8,128)(2,1)} %param.5) | data formatting | bytes 33554432 | tf_op jit(solution)/shard_map/reshape | solution.py:18
  77.5 155.8 %all-to-all-done = bf16[4,16,16,8192]{3,2,0,1:T(8,128)(2,1)} async-done(((bf16[4,16,16,8192]{3,2,0,1:T(8,128)(2,1)}), bf16[4,16,16,8192]{3,2,0,1:T(8,128)(2,1)}, u32[]{:S(2)}, u32[]{:S(2)}) %all-to-all-start) | async-done | bytes 16777248 | tf_op jit(solution)/shard_map/all_to_all | solution.py:24
  233.3 7.4 %broadcast_compare_fusion = pred[4,16,16,8192]{3,2,0,1:T(8,128)(4,1)S(1)} fusion(bf16[4,16,16,8192]{3,2,0,1:T(8,128)(2,1)} %all-to-all-done), kind=kLoop, calls=%fused_computation.15 | loop fusion | flops 8388608 | bytes 25165824 | tf_op jit(solution)/shard_map/gt | solution.py:29
  240.7 0.0 copy-start.1
  240.7 25.3 %copy.71 = pred[4,4,4,16,8192]{4,0,1,3,2:T(4,128)(4,1)} copy(pred[4,4,4,16,8192]{4,3,0,2,1:T(8,128)(4,1)S(1)} %bitcast.54) | data formatting | bytes 16777216 | tf_op jit(solution)/shard_map/gt | solution.py:29
  265.9 20.9 %gt.15 = pred[16,4,16,8192]{3,0,2,1:T(8,128)(4,1)} reshape(pred[4,4,4,16,8192]{4,1,0,3,2:T(4,128)(4,1)} %bitcast.55) | data formatting | bytes 16777216 | tf_op jit(solution)/shard_map/gt | solution.py:29
  286.8 0.0 copy-done.1
  286.8 24.9 %fusion = bf16[16,4,16,8192]{3,0,2,1:T(8,128)(2,1)} fusion(pred[16,4,16,8192]{3,0,2,1:T(8,128)(4,1)} %gt.15, bf16[4,16,16,256]{3,2,1,0:T(8,128)(2,1)S(1)} %bitcast.62, bf16[8192,4,256,1]{2,1,0,3:T(4,128)(2,1)} %bitcast.58), kind=kOutput, calls=%fused_computation.1 | convolution fusion | flops 4311744512 | bytes 42467328 | tf_op jit(solution)/shard_map/tco,cjbo->bcjt/dot_general | solution.py:28
  311.7 18.5 %copy.33 = bf16[16,4,16,8192]{3,2,1,0:T(8,128)(2,1)} copy(bf16[16,4,16,8192]{3,0,2,1:T(8,128)(2,1)} %fusion) | data formatting | bytes 33554432 | tf_op jit(solution)/shard_map/convert_element_type | solution.py:29
  330.1 7.1 %all-to-all-start.1 = ((bf16[16,4,16,8192]{3,2,1,0:T(8,128)(2,1)}), bf16[16,4,16,8192]{3,2,1,0:T(8,128)(2,1)}, u32[]{:S(2)}, u32[]{:S(2)}) async-start(bf16[16,4,16,8192]{3,2,1,0:T(8,128)(2,1)} %copy.33), calls=%async_computation.1 | async-start | bytes 33554432 | tf_op jit(solution)/shard_map/all_to_all | solution.py:30
  337.2 0.2 all-reduce.3.cloned.1.call-start
  337.5 8.0 %broadcast_maximum_fusion = bf16[4,16,16,8192]{3,2,0,1:T(8,128)(2,1)S(1)} fusion(bf16[4,16,16,8192]{3,2,0,1:T(8,128)(2,1)} %all-to-all-done), kind=kLoop, calls=%fused_computation.14 | loop fusion | flops 8388608 | bytes 33554432 | tf_op jit(solution)/shard_map/max | solution.py:25
  345.4 6.6 %copy.37 = bf16[4,4,4,16,8192]{4,3,0,1,2:T(8,128)(2,1)} copy(bf16[4,4,4,16,8192]{4,3,0,2,1:T(8,128)(2,1)S(1)} %bitcast.51) | data formatting | bytes 33554432 | tf_op jit(solution)/shard_map/max | solution.py:25
  352.0 168.3 %all-to-all-done.1 = bf16[16,4,16,8192]{3,2,1,0:T(8,128)(2,1)} async-done(((bf16[16,4,16,8192]{3,2,1,0:T(8,128)(2,1)}), bf16[16,4,16,8192]{3,2,1,0:T(8,128)(2,1)}, u32[]{:S(2)}, u32[]{:S(2)}) %all-to-all-start.1) | async-done | bytes 16777248 | tf_op jit(solution)/shard_map/all_to_all | solution.py:30
  520.3 13.9 %copy.34 = bf16[4,4,4,16,8192]{4,3,2,0,1:T(8,128)(2,1)} copy(bf16[4,4,4,16,8192]{4,3,2,1,0:T(8,128)(2,1)} %bitcast.6) | data formatting | bytes 33554432 | tf_op jit(solution)/shard_map/all_to_all | solution.py:30
  534.2 12.9 %fusion.22 = f32[4,256,256]{1,2,0:T(8,128)S(1)} fusion(bf16[4,256,8192]{2,1,0:T(8,128)(2,1)} %bitcast.49, bf16[1024,4,8,256]{3,2,1,0:T(8,128)(2,1)} %bitcast.57), kind=kOutput, calls=%fused_computation.19 | convolution fusion | flops 4295229440 | bytes 34603008 | tf_op jit(solution)/shard_map/tbi,bjt->bij/dot_general | solution.py:33
  547.1 1.4 copy.36
  548.5 0.0 all-reduce.3.cloned.1.call-update
  548.5 0.0 reduce-scatter.2.cloned.1.call-start
  548.6 0.0 copy-start.2
  548.6 13.1 %fusion.16 = f32[4,16,16,256]{3,1,2,0:T(8,128)S(1)} fusion(bf16[16,4,16,8192]{3,2,0,1:T(8,128)(2,1)} %bitcast.60, bf16[8192,4,256,1]{2,1,0,3:T(4,128)(2,1)} %bitcast.59), kind=kOutput, calls=%fused_computation.17 | convolution fusion | flops 4295229440 | bytes 34603008 | tf_op jit(solution)/shard_map/bcjt,tco->cjbo/dot_general | solution.py:26
  561.7 1.6 copy.39
  563.3 0.0 reduce-scatter.2.cloned.1.call-update
  563.3 0.0 copy-done.2
  563.4 0.6 dynamic-slice
  564.6 13.9 %convolution_convert_fusion = bf16[4,8192,256]{1,2,0:T(8,128)(2,1)} fusion(bf16[4,256,256]{2,1,0:T(8,128)(2,1)S(1)} %copy-done, bf16[4,256,8192]{2,1,0:T(8,128)(2,1)} %bitcast.50), kind=kOutput, calls=%fused_computation.8 | convolution fusion | flops 4303355904 | bytes 34078720 | tf_op jit(solution)/shard_map/bjt,bij->tbi/dot_general | solution.py:36
  578.5 22.5 %copy.40 = bf16[8192,1024]{1,0:T(8,128)(2,1)} copy(bf16[8192,1024]{0,1:T(8,128)(2,1)} %bitcast.52) | data formatting | bytes 33554432
  601.0 0.7 all-reduce.3.cloned.1.call-done
  601.7 1.0 constant_dynamic-slice_fusion
  602.6 0.8 copy.41
  603.4 27.8 %reduce-scatter.2.cloned.1.call-done = f32[4,64,256]{2,1,0:T(8,128)} async-done(((f32[4,256,256]{2,1,0:T(8,128)}), f32[4,64,256]{2,1,0:T(8,128)}) %reduce-scatter.2.cloned.1.call-update) | async-done | bytes 262160 | tf_op jit(solution)/shard_map/reduce_scatter | solution.py:40
Async XLA Ops:
  7.2 1.0 copy-start
  42.6 190.6 %all-to-all-start = ((bf16[4,16,16,8192]{3,2,0,1:T(8,128)(2,1)}), bf16[4,16,16,8192]{3,2,0,1:T(8,128)(2,1)}, u32[]{:S(2)}, u32[]{:S(2)}) async-start(bf16[4,16,16,8192]{3,2,0,1:T(8,128)(2,1)} %copy.30), calls=%async_computation | async-start | bytes 33554432 | tf_op jit(solution)/shard_map/all_to_all | solution.py:24
  240.7 46.1 %copy-start.1 = (bf16[4,256,256]{2,1,0:T(8,128)(2,1)S(1)}, bf16[4,256,256]{2,1,0:T(8,128)(2,1)}, u32[]{:S(2)}) copy-start(bf16[4,256,256]{2,1,0:T(8,128)(2,1)} %param.7) | copy-start | bytes 1572868
  330.1 190.2 %all-to-all-start.1 = ((bf16[16,4,16,8192]{3,2,1,0:T(8,128)(2,1)}), bf16[16,4,16,8192]{3,2,1,0:T(8,128)(2,1)}, u32[]{:S(2)}, u32[]{:S(2)}) async-start(bf16[16,4,16,8192]{3,2,1,0:T(8,128)(2,1)} %copy.33), calls=%async_computation.1 | async-start | bytes 33554432 | tf_op jit(solution)/shard_map/all_to_all | solution.py:30
  337.2 264.4 %all-reduce.3.cloned.1.call-start = ((), (), s32[]{:S(2)}) async-start(), calls=%async_computation.4 | async-start | bytes 2097152
  548.5 82.6 %reduce-scatter.2.cloned.1.call-start = ((), (), s32[]{:S(2)}) async-start(), calls=%async_computation.3 | async-start | bytes 1310720 | tf_op jit(solution)/shard_map/reduce_scatter | solution.py:40
  548.6 14.8 %copy-start.2 = (u32[32]{0:T(128)S(1)}, u32[32]{0:T(128)}, u32[]{:S(2)}) copy-start(u32[32]{0:T(128)} %constant.8) | copy-start | bytes 388
Sparse Core Ops, SparseCore 0:
  548.6 52.9 all-reduce.2
  604.6 26.5 reduce-scatter.1
where the time goes:
time: 641 us; the launch traced here: 638 us
  waiting for transfers between devices  353 us (55%)
  local copies, waits for them, and re-layouts  156 us (24%)
  matrix products  85.4 us (13%)
  other arithmetic  15.3 us (2%)
  between operations  14.8 us (2%)
  starting transfers between devices  14.3 us (2%)
    all_to_all x1, waiting for transfers between devices, shards(): lax.all_to_all(masked, 'tensor', split_axis=0, concat_axis=1, tiled=True)  168 us
    all_to_all x1, waiting for transfers between devices, shards(): lax.all_to_all(hidden, 'tensor', split_axis=1, concat_axis=0, tiled=True)  156 us
    gt x2, local copies, waits for them, and re-layouts, shards(): moved > 0  46.1 us
    reshape x1, local copies, waits for them, and re-layouts, shards(): upstream = cotangent.reshape(tok_rows, blk_local, blk_width)  27.9 us
    reduce_scatter x1, waiting for transfers between devices, shards(): lax.psum_scatter(second_term, 'dp', scatter_dimension=1, tiled=True)  27.8 us
    unnamed x10, local copies, waits for them, and re-layouts  25.8 us
    dot_general x1, matrix products, shards(): jnp.einsum('tco,cjbo->bcjt', upstream, second_view, preferred_element_typ...  24.9 us
    dot_general x1, matrix products, shards(): jnp.einsum('tbi,bij->bjt', inputs, w_first, preferred_element_type=jnp.fl...  20.5 us
  transfers between devices with their start and end apart: 4, of which 4 were waited for; matrix products, arithmetic and copies ran while one was open for 15% of the time, Pallas kernels for 0%

commit v1 on v0

--- a/solution.py
+++ b/solution.py
@@ -21,7 +21,9 @@
     )
     hidden = hidden.reshape(blk_local, NB, sub_width, tok_rows)
     second_view = w_second.reshape(blk_local, sub_width, NB, blk_width)
-    moved = lax.all_to_all(hidden, "tensor", split_axis=1, concat_axis=0, tiled=True)
+    cells = jnp.split(hidden, lax.axis_size("tensor"), axis=1)
+    incoming = lax.all_to_all(jnp.stack(cells), "tensor", 0, 0)
+    moved = jnp.concatenate(incoming, axis=0)
     active = jnp.maximum(moved, jnp.zeros((), jnp.bfloat16))
     second_term = jnp.einsum("bcjt,tco->cjbo", active, upstream, preferred_element_type=jnp.float32)
     second_term = second_term.reshape(blk_local, blk_width, blk_width) * grad_scale

time: 641 us -> 605 us (0.944)
  local copies, waits for them, and re-layouts: 156 us -> 102 us
  other arithmetic: 15.3 us -> 25.5 us
  matrix products: 85.4 us -> 93.5 us
    gt x2 -> x0, local copies, waits for them, and re-layouts: 46.1 us -> none  [shards(): moved > 0]
    reshape x1 -> x0, local copies, waits for them, and re-layouts: 13.9 us -> none  [shards(): hidden = hidden.reshape(blk_local, NB, sub_width, tok_rows)]
    dot_general x1, matrix products: 24.9 us -> 33 us  [shards(): jnp.einsum('tco,cjbo->bcjt', upstream, second_view, preferred_element_typ...]
    another operation x0 -> x1, other arithmetic: none -> 7.03 us  [shards(): incoming = lax.all_to_all(jnp.stack(cells), 'tensor', 0, 0)]
    another operation x0 -> x1, local copies, waits for them, and re-layouts: none -> 6.49 us  [shards(): incoming = lax.all_to_all(jnp.stack(cells), 'tensor', 0, 0)]
  transfers between devices with their start and end apart: 4 -> 4, of which waited for: 4 -> 4; matrix products, arithmetic and copies ran while one was open for 15% -> 16% of each run, Pallas kernels for 0% -> 0%
where the time goes in v1:
time: 605 us; the launch traced here: 603 us
  waiting for transfers between devices  352 us (58%)
  local copies, waits for them, and re-layouts  102 us (17%)
  matrix products  93.5 us (15%)
  other arithmetic  25.5 us (4%)
  between operations  14.8 us (2%)
  starting transfers between devices  14.6 us (2%)
    all_to_all x1, waiting for transfers between devices, shards(): lax.all_to_all(masked, 'tensor', split_axis=0, concat_axis=1, tiled=True)  168 us
    all_to_all x1, waiting for transfers between devices, shards(): incoming = lax.all_to_all(jnp.stack(cells), 'tensor', 0, 0)  156 us
    dot_general x1, matrix products, shards(): jnp.einsum('tco,cjbo->bcjt', upstream, second_view, preferred_element_typ...  33 us
    reshape x1, local copies, waits for them, and re-layouts, shards(): upstream = cotangent.reshape(tok_rows, blk_local, blk_width)  27.9 us
    reduce_scatter x1, waiting for transfers between devices, shards(): lax.psum_scatter(second_term, 'dp', scatter_dimension=1, tiled=True)  27.8 us
    unnamed x10, local copies, waits for them, and re-layouts  25.8 us
    dot_general x1, matrix products, shards(): jnp.einsum('tbi,bij->bjt', inputs, w_first, preferred_element_type=jnp.fl...  20.5 us
    convert_element_type x1, local copies, waits for them, and re-layouts, shards(): jnp.where(moved > 0, backed, jnp.zeros((), jnp.float32))  18.5 us
  transfers between devices with their start and end apart: 4, of which 4 were waited for; matrix products, arithmetic and copies ran while one was open for 16% of the time, Pallas kernels for 0%

profile of v1, /device:TPU:0, one launch (start us, length us, event | category | flops | bytes accessed | tf_op | source)
XLA Modules:
  0.0 602.8 jit_solution(13479205193895212360)
XLA Ops:
  7.2 0.0 copy-start
  7.2 1.0 copy-done
  8.2 20.5 %fusion.5 = bf16[4,256,8192]{2,1,0:T(8,128)(2,1)} fusion(bf16[4,256,256]{2,1,0:T(8,128)(2,1)S(1)} %copy-done, bf16[1024,4,8,256]{3,2,1,0:T(8,128)(2,1)} %bitcast.53), kind=kOutput, calls=%fused_computation.7 | convolution fusion | flops 4303355904 | bytes 34078720 | tf_op jit(solution)/shard_map/tbi,bij->bjt/dot_general | solution.py:19
  28.8 6.5 %slice_bitcast_fusion.3 = (bf16[1,4,4,16,8192]{4,3,2,1,0:T(8,128)(2,1)S(1)}, bf16[1,4,4,16,8192]{4,3,2,1,0:T(8,128)(2,1)S(1)}, bf16[1,4,4,16,8192]{4,3,2,1,0:T(8,128)(2,1)S(1)}, bf16[1,4,4,16,8192]{4,3,2,1,0:T(8,128)(2,1)S(1)}) fusion(bf16[4,16,16,8192]{3,2,1,0:T(8,128)(2,1)} %bitcast.51), kind=kLoop, calls=%fused_computation.19 | loop fusion | bytes 33554432 | tf_op jit(solution)/shard_map/stack | solution.py:25
  35.3 7.0 %pad_maximum_fusion = bf16[4,4,4,16,8192]{4,3,2,1,0:T(8,128)(2,1)} fusion(bf16[1,4,4,16,8192]{4,3,2,1,0:T(8,128)(2,1)S(1)} %get-tuple-element.13, bf16[1,4,4,16,8192]{4,3,2,1,0:T(8,128)(2,1)S(1)} %get-tuple-element.14, bf16[1,4,4,16,8192]{4,3,2,1,0:T(8,128)(2,1)S(1)} %get-tuple-element.15, bf16[1,4,4,16,8192]{4,3,2,1,0:T(8,128)(2,1)S(1)} %get-tuple-element.12), kind=kLoop, calls=%fused_computation.6 | loop fusion | flops 25165824 | bytes 33554432 | tf_op jit(solution)/shard_map/stack | solution.py:25
  42.3 7.2 %all-to-all-start = ((bf16[4,4,4,16,8192]{4,3,2,1,0:T(8,128)(2,1)}), bf16[4,4,4,16,8192]{4,3,2,1,0:T(8,128)(2,1)}, u32[]{:S(2)}, u32[]{:S(2)}) async-start(bf16[4,4,4,16,8192]{4,3,2,1,0:T(8,128)(2,1)} %pad_maximum_fusion), calls=%async_computation | async-start | bytes 33554432 | tf_op jit(solution)/shard_map/all_to_all | solution.py:25
  49.4 27.9 %reshape.36 = bf16[8192,4,256]{2,1,0:T(4,128)(2,1)} reshape(bf16[8192,1024]{1,0:T(8,128)(2,1)} %param.5) | data formatting | bytes 33554432 | tf_op jit(solution)/shard_map/reshape | solution.py:18
  77.3 0.0 copy-start.1
  77.3 155.7 %all-to-all-done = bf16[4,4,4,16,8192]{4,3,2,1,0:T(8,128)(2,1)} async-done(((bf16[4,4,4,16,8192]{4,3,2,1,0:T(8,128)(2,1)}), bf16[4,4,4,16,8192]{4,3,2,1,0:T(8,128)(2,1)}, u32[]{:S(2)}, u32[]{:S(2)}) %all-to-all-start) | async-done | bytes 16777248 | tf_op jit(solution)/shard_map/all_to_all | solution.py:25
  233.1 10.4 %broadcast_compare_fusion = pred[4,4,4,16,8192]{4,3,2,1,0:T(8,128)(4,1)} fusion(bf16[4,4,4,16,8192]{4,3,2,1,0:T(8,128)(2,1)} %all-to-all-done), kind=kLoop, calls=%fused_computation.15 | loop fusion | flops 8388608 | bytes 25165824 | tf_op jit(solution)/shard_map/gt | solution.py:31
  243.5 0.0 copy-done.1
  243.5 33.0 %fusion = bf16[16,4,16,8192]{3,0,2,1:T(8,128)(2,1)} fusion(pred[16,4,16,8192]{3,2,1,0:T(8,128)(4,1)} %bitcast.58, bf16[4,16,16,256]{3,2,1,0:T(8,128)(2,1)S(1)} %bitcast.60, bf16[8192,4,256,1]{2,1,0,3:T(4,128)(2,1)} %bitcast.55), kind=kOutput, calls=%fused_computation.1 | convolution fusion | flops 4311744512 | bytes 42467328 | tf_op jit(solution)/shard_map/tco,cjbo->bcjt/dot_general | solution.py:30
  276.5 18.5 %copy.32 = bf16[16,4,16,8192]{3,2,1,0:T(8,128)(2,1)} copy(bf16[16,4,16,8192]{3,0,2,1:T(8,128)(2,1)} %fusion) | data formatting | bytes 33554432 | tf_op jit(solution)/shard_map/convert_element_type | solution.py:31
  295.0 7.1 %all-to-all-start.1 = ((bf16[16,4,16,8192]{3,2,1,0:T(8,128)(2,1)}), bf16[16,4,16,8192]{3,2,1,0:T(8,128)(2,1)}, u32[]{:S(2)}, u32[]{:S(2)}) async-start(bf16[16,4,16,8192]{3,2,1,0:T(8,128)(2,1)} %copy.32), calls=%async_computation.1 | async-start | bytes 33554432 | tf_op jit(solution)/shard_map/all_to_all | solution.py:32
  302.1 0.3 all-reduce.3.cloned.1.call-start
  302.4 8.0 %broadcast_maximum_fusion = bf16[4,4,4,16,8192]{4,3,2,1,0:T(8,128)(2,1)S(1)} fusion(bf16[4,4,4,16,8192]{4,3,2,1,0:T(8,128)(2,1)} %all-to-all-done), kind=kLoop, calls=%fused_computation.14 | loop fusion | flops 8388608 | bytes 33554432 | tf_op jit(solution)/shard_map/max | solution.py:27
  310.4 6.5 %copy.36 = bf16[4,4,4,16,8192]{4,3,1,0,2:T(8,128)(2,1)} copy(bf16[4,4,4,16,8192]{4,3,2,1,0:T(8,128)(2,1)S(1)} %broadcast_maximum_fusion) | data formatting | bytes 33554432 | tf_op jit(solution)/shard_map/max | solution.py:27
  316.9 168.2 %all-to-all-done.1 = bf16[16,4,16,8192]{3,2,1,0:T(8,128)(2,1)} async-done(((bf16[16,4,16,8192]{3,2,1,0:T(8,128)(2,1)}), bf16[16,4,16,8192]{3,2,1,0:T(8,128)(2,1)}, u32[]{:S(2)}, u32[]{:S(2)}) %all-to-all-start.1) | async-done | bytes 16777248 | tf_op jit(solution)/shard_map/all_to_all | solution.py:32
  485.2 14.0 %copy.33 = bf16[4,4,4,16,8192]{4,3,2,0,1:T(8,128)(2,1)} copy(bf16[4,4,4,16,8192]{4,3,2,1,0:T(8,128)(2,1)} %bitcast.9) | data formatting | bytes 33554432 | tf_op jit(solution)/shard_map/all_to_all | solution.py:32
  499.2 12.9 %fusion.22 = f32[4,256,256]{1,2,0:T(8,128)S(1)} fusion(bf16[4,256,8192]{2,1,0:T(8,128)(2,1)} %bitcast.49, bf16[1024,4,8,256]{3,2,1,0:T(8,128)(2,1)} %bitcast.54), kind=kOutput, calls=%fused_computation.23 | convolution fusion | flops 4295229440 | bytes 34603008 | tf_op jit(solution)/shard_map/tbi,bjt->bij/dot_general | solution.py:35
  512.1 1.4 copy.35
  513.5 0.0 all-reduce.3.cloned.1.call-update
  513.5 0.0 reduce-scatter.2.cloned.1.call-start
  513.5 0.0 copy-start.2
  513.6 13.1 %fusion.16 = f32[4,16,16,256]{3,1,2,0:T(8,128)S(1)} fusion(bf16[16,4,16,8192]{3,2,0,1:T(8,128)(2,1)} %bitcast.57, bf16[8192,4,256,1]{2,1,0,3:T(4,128)(2,1)} %bitcast.56), kind=kOutput, calls=%fused_computation.21 | convolution fusion | flops 4295229440 | bytes 34603008 | tf_op jit(solution)/shard_map/bcjt,tco->cjbo/dot_general | solution.py:28
  526.7 1.6 copy.38
  528.3 0.0 reduce-scatter.2.cloned.1.call-update
  528.3 0.0 copy-done.2
  528.3 0.6 dynamic-slice
  529.6 13.9 %convolution_convert_fusion = bf16[4,8192,256]{1,2,0:T(8,128)(2,1)} fusion(bf16[4,256,256]{2,1,0:T(8,128)(2,1)S(1)} %copy-done, bf16[4,256,8192]{2,1,0:T(8,128)(2,1)} %bitcast.50), kind=kOutput, calls=%fused_computation.8 | convolution fusion | flops 4303355904 | bytes 34078720 | tf_op jit(solution)/shard_map/bjt,bij->tbi/dot_general | solution.py:38
  543.5 22.5 %copy.39 = bf16[8192,1024]{1,0:T(8,128)(2,1)} copy(bf16[8192,1024]{0,1:T(8,128)(2,1)} %bitcast.52) | data formatting | bytes 33554432
  566.0 0.5 all-reduce.3.cloned.1.call-done
  566.5 1.0 constant_dynamic-slice_fusion
  567.4 0.8 copy.40
  568.2 27.8 %reduce-scatter.2.cloned.1.call-done = f32[4,64,256]{2,1,0:T(8,128)} async-done(((f32[4,256,256]{2,1,0:T(8,128)}), f32[4,64,256]{2,1,0:T(8,128)}) %reduce-scatter.2.cloned.1.call-update) | async-done | bytes 262160 | tf_op jit(solution)/shard_map/reduce_scatter | solution.py:42
Async XLA Ops:
  7.2 1.0 copy-start
  42.3 190.8 %all-to-all-start = ((bf16[4,4,4,16,8192]{4,3,2,1,0:T(8,128)(2,1)}), bf16[4,4,4,16,8192]{4,3,2,1,0:T(8,128)(2,1)}, u32[]{:S(2)}, u32[]{:S(2)}) async-start(bf16[4,4,4,16,8192]{4,3,2,1,0:T(8,128)(2,1)} %pad_maximum_fusion), calls=%async_computation | async-start | bytes 33554432 | tf_op jit(solution)/shard_map/all_to_all | solution.py:25
  77.3 166.2 %copy-start.1 = (bf16[4,256,256]{2,1,0:T(8,128)(2,1)S(1)}, bf16[4,256,256]{2,1,0:T(8,128)(2,1)}, u32[]{:S(2)}) copy-start(bf16[4,256,256]{2,1,0:T(8,128)(2,1)} %param.7) | copy-start | bytes 1572868
  295.0 190.2 %all-to-all-start.1 = ((bf16[16,4,16,8192]{3,2,1,0:T(8,128)(2,1)}), bf16[16,4,16,8192]{3,2,1,0:T(8,128)(2,1)}, u32[]{:S(2)}, u32[]{:S(2)}) async-start(bf16[16,4,16,8192]{3,2,1,0:T(8,128)(2,1)} %copy.32), calls=%async_computation.1 | async-start | bytes 33554432 | tf_op jit(solution)/shard_map/all_to_all | solution.py:32
  302.1 264.3 %all-reduce.3.cloned.1.call-start = ((), (), s32[]{:S(2)}) async-start(), calls=%async_computation.4 | async-start | bytes 2097152
  513.5 82.5 %reduce-scatter.2.cloned.1.call-start = ((), (), s32[]{:S(2)}) async-start(), calls=%async_computation.3 | async-start | bytes 1310720 | tf_op jit(solution)/shard_map/reduce_scatter | solution.py:42
  513.5 14.8 %copy-start.2 = (u32[32]{0:T(128)S(1)}, u32[32]{0:T(128)}, u32[]{:S(2)}) copy-start(u32[32]{0:T(128)} %constant.8) | copy-start | bytes 388
Sparse Core Ops, SparseCore 0:
  513.6 52.7 all-reduce.2
  569.4 26.5 reduce-scatter.1
